TPU v7x, 32 devices: a whole 2x2x4 slice. The times are simulated.
32 devices in a mesh: lon: 4 (over x, core), lat: 8 (over z, y).
Axes of the slice: x: 2, y: 2, z: 4, core: 2. Of those that a mesh axis runs over, the one named last changes fastest.
Arguments:
- prognostic: float32 [4, 16, 192, 1536], P(None, None, 'lat', 'lon'), may hold values from -6 to 6
- tracers: float32 [4, 16, 192, 1536], P(None, None, 'lat', 'lon'), may hold values from -6 to 6
- zonal_courant: float32 [16, 192, 1536], P(None, 'lat', 'lon'), may hold values from -0.45 to 0.45
- meridional_courant: float32 [16, 192, 1536], P(None, 'lat', 'lon'), may hold values from -0.45 to 0.45
- filter_band: int32 [192], P('lat'), may hold values from 96 to 768, as said below
- dep_owner: int32 [192, 2], P('lat'), may hold values from 0 to 7, as said below
- dep_row: int32 [192, 2], P('lat'), may hold values from 0 to 23
- dep_weight: float32 [192, 2], P('lat'), may hold values from 0 to 1, as said below
Outputs:
- new_prognostic: float32 [4, 16, 192, 1536], P(None, None, 'lat', 'lon')
- new_tracers: float32 [4, 16, 192, 1536], P(None, None, 'lat', 'lon')
Inputs may be any that keep to these rules, and one draw needn't show every extreme that they name: `filter_band`: rows within 24 of either pole hold values below 768; all other rows hold 768. `dep_owner`: among the 48 entries of one band, at most 12 name the same owner band, and some owner is named exactly 12 times; the owners a band names are the bands nearest to it, distance counted across either pole. `dep_weight`: Positive; the 2 weights of a row sum to 1.
All inputs are finite; a program needn't handle non-finite values.
Results may differ from a plain program's by a relative error of at most 0.00007.
Values sent between devices are 32-bit elements; how exact they have to be, the bound alone decides.
No kernel may reach another device: no remote copies, remote signals or barrier semaphores. Data moves between devices by JAX's collectives and lax.ppermute only.
A program may use at most 128 MiB of HBM per device.

v0:
```python
import math
import jax
import jax.numpy as jnp
from jax import lax
from jax.sharding import PartitionSpec as P

PRECISE = lax.Precision.HIGHEST


def padded(value, sides, width, wrap):
    for axis, dim in sides:
        size, length = (lax.axis_size(axis), value.shape[dim])
        up = [(i, (i + 1) % size) for i in range(size if wrap else size - 1)]
        down = [(j, i) for i, j in up]
        last = lax.slice_in_dim(value, length - width, length, axis=dim)
        first = lax.slice_in_dim(value, 0, width, axis=dim)
        before = lax.ppermute(last, axis, up)
        after = lax.ppermute(first, axis, down)
        value = jnp.concatenate([before, value, after], axis=dim)
    return value


def face_flux(values, speeds, axis):
    count = values.shape[axis] - 2
    left_cells = lax.slice_in_dim(values, 0, count + 1, axis=axis)
    right_cells = lax.slice_in_dim(values, 1, count + 2, axis=axis)
    courant = lax.slice_in_dim(speeds, 0, count + 1, axis=axis)
    return 0.5 * courant * (left_cells + right_cells) - 0.5 * courant * courant * (
        right_cells - left_cells
    )


def column_factors(band_rows, length):
    column = jnp.arange(length, dtype=jnp.int32)
    half_length = length // 2
    frequency = jnp.where(column <= half_length, column, column - half_length)
    single = (column == 0) | (column == half_length)
    weights = jnp.where(single, 1.0 / length, 2.0 / length).astype(jnp.float32)
    ratios = (
        band_rows.astype(jnp.float32)[:, None]
        / jnp.maximum(frequency, 1).astype(jnp.float32)[None, :]
    )
    damping = jnp.minimum(1.0, ratios * ratios)
    return (damping - 1.0) * weights[None, :]


def circle_basis(length):
    half_length = length // 2
    column = jnp.arange(length, dtype=jnp.int32)
    frequency = jnp.where(column <= half_length, column, column - half_length)
    low_count = 64
    high_count = length // low_count
    low = jnp.arange(low_count, dtype=jnp.int32)
    high = jnp.arange(high_count, dtype=jnp.int32) * low_count
    scale = 2.0 * math.pi / length
    low_angle = scale * (low[:, None] * frequency[None, :] % length).astype(jnp.float32)
    high_angle = scale * (high[:, None] * frequency[None, :] % length).astype(jnp.float32)
    low_cos, low_sin = (jnp.cos(low_angle), jnp.sin(low_angle))
    high_cos, high_sin = (jnp.cos(high_angle), jnp.sin(high_angle))
    cos_part = high_cos[:, None] * low_cos[None] - high_sin[:, None] * low_sin[None]
    sin_part = high_sin[:, None] * low_cos[None] + high_cos[:, None] * low_sin[None]
    basis = jnp.where((column <= half_length)[None, None, :], cos_part, sin_part)
    return basis.reshape(length, length)


def polar_filter(values, band_rows):
    fields, levels, rows, block_cells = values.shape
    parts = lax.axis_size("lon")
    length = block_cells * parts
    flat = values.reshape(fields * levels * rows, block_cells)
    circles = lax.all_to_all(flat, "lon", split_axis=0, concat_axis=1, tiled=True)
    basis_table = circle_basis(length)
    spectrum = jnp.dot(circles, basis_table, precision=PRECISE)
    factors = column_factors(band_rows, length)
    circle_rows = circles.shape[0]
    scaled = (spectrum.reshape(circle_rows // rows, rows, length) * factors[None]).reshape(
        circle_rows, length
    )
    change = lax.dot_general(scaled, basis_table, (((1,), (1,)), ((), ())), precision=PRECISE)
    back = lax.all_to_all(change, "lon", split_axis=1, concat_axis=0, tiled=True)
    return values + back.reshape(values.shape)


def departure_terms(tracers, dep_owner, dep_row, dep_weight):
    band_count = lax.axis_size("lat")
    row_count, link_count = dep_owner.shape
    entries = row_count * link_count
    capacity = max(2, -(-2 * entries // band_count))
    owner_ids = dep_owner.reshape(entries)
    source = dep_row.reshape(entries)
    positions = jnp.arange(entries)
    earlier = (owner_ids[:, None] == owner_ids[None, :]) & (positions[None, :] < positions[:, None])
    slot_ids = jnp.sum(earlier.astype(jnp.int32), axis=1)
    band_ids = jnp.arange(band_count, dtype=jnp.int32)
    slot_range = jnp.arange(capacity, dtype=jnp.int32)
    matches = (owner_ids[:, None, None] == band_ids[None, :, None]) & (
        slot_ids[:, None, None] == slot_range[None, None, :]
    )
    request = jnp.sum(jnp.where(matches, source[:, None, None], 0), axis=0)
    wanted = lax.all_to_all(request, "lat", split_axis=0, concat_axis=0, tiled=True)
    by_row = jnp.transpose(tracers, (2, 0, 1, 3))
    outgoing = by_row[wanted]
    incoming = lax.all_to_all(outgoing, "lat", split_axis=0, concat_axis=0, tiled=True)
    stacked_rows = incoming.reshape((band_count * capacity,) + incoming.shape[2:])
    picked = stacked_rows[owner_ids * capacity + slot_ids].reshape(
        (row_count, link_count) + stacked_rows.shape[1:]
    )
    summed = dep_weight[:, 0][:, None, None, None] * picked[:, 0]
    summed = summed + dep_weight[:, 1][:, None, None, None] * picked[:, 1]
    return jnp.transpose(summed, (1, 2, 0, 3))


def body(
    prognostic,
    tracers,
    zonal_courant,
    meridional_courant,
    filter_band,
    dep_owner,
    dep_row,
    dep_weight,
):
    row_count = prognostic.shape[2]
    departed = departure_terms(tracers, dep_owner, dep_row, dep_weight)
    lon_padded = padded(
        jnp.concatenate([prognostic, zonal_courant[None]], axis=0), (("lon", 3),), 1, True
    )
    zonal_flux = face_flux(lon_padded[:-1], lon_padded[-1:], 3)
    lat_padded = padded(
        jnp.concatenate([prognostic, meridional_courant[None]], axis=0), (("lat", 2),), 1, False
    )
    merid_flux = face_flux(lat_padded[:-1], lat_padded[-1:], 2)
    total_rows = row_count * lax.axis_size("lat")
    face_rows = lax.axis_index("lat") * row_count + jnp.arange(row_count + 1) - 1
    merid_flux = jnp.where(
        (face_rows == total_rows - 1)[None, None, :, None], jnp.float32(0.0), merid_flux
    )
    advected = (
        prognostic
        - (zonal_flux[..., 1:] - zonal_flux[..., :-1])
        - (merid_flux[:, :, 1:] - merid_flux[:, :, :-1])
    )
    new_prognostic = polar_filter(advected, filter_band)
    return (new_prognostic, departed)


def solution(mesh):
    return jax.shard_map(
        body,
        mesh=mesh,
        in_specs=(
            P(None, None, "lat", "lon"),
            P(None, None, "lat", "lon"),
            P(None, "lat", "lon"),
            P(None, "lat", "lon"),
            P("lat"),
            P("lat", None),
            P("lat", None),
            P("lat", None),
        ),
        out_specs=(P(None, None, "lat", "lon"), P(None, None, "lat", "lon")),
        check_vma=False,
    )
```

profile of v0, /device:TPU:0, one launch (start us, length us, event | category | flops | bytes accessed | tf_op | source)
XLA Modules:
  0.0 364.4 jit_solution(3108932577473310589)
XLA Ops:
  0.7 3.3 pad_maximum_fusion.8
  4.0 1.8 copy.57
  6.2 1.7 copy.59
  7.9 2.0 collective-permute-start.1
  10.8 4.9 %collective-permute-start.2 = (f32[5,16,1,384]{3,1,2,0:T(8,128)}, f32[5,16,1,384]{3,1,2,0:T(8,128)}, u32[]{:S(2)}, u32[]{:S(2)}) collective-permute-start(f32[5,16,1,384]{3,1,2,0:T(8,128)} %copy.61), channel_id=1, source_target_pairs={{0,1},{1,2},{2,3},{3,4},{4,5},{5,6},{6,7},{8,9},{9,10},{10,11},{11... | collective-permute-start | bytes 368648 | tf_op jit(solution)/shard_map/ppermute | solution.py:17
  16.3 1.3 collective-permute-start.3
  19.5 1.3 copy.58
  20.8 2.2 multiply_bitcast_fusion.1
  24.0 2.3 copy.60
  26.3 2.7 multiply_subtract_fusion
  30.4 1.0 copy.64
  31.4 1.2 subtract_select_fusion
  32.6 2.3 fusion.4
  34.9 3.6 all-to-all-start
  39.9 1.6 fusion.14
  41.5 5.8 %add_select_fusion = f32[24,64,1536]{2,1,0:T(8,128)} fusion(f32[64,1536]{1,0:T(8,128)S(1)} %get-tuple-element.21, f32[24,1536]{1,0:T(8,128)S(1)} %get-tuple-element.19, f32[64,1536]{1,0:T(8,128)S(1)} %get-tuple-element.20, f32[24,1536]{1,0:T(8,128)S(1)} %get-tuple-element.18, pred[1536]{0:T(1024)(128)(4,1)S(1)} %iota_compare_fusion.4), kind=kLoop, calls=%fused_computation.2 | loop fusion | flops 16515072 | bytes 10520064 | tf_op jit(solution)/shard_map/jit(_where)/select_n | solution.py:62
  47.3 19.7 %all-to-all-done = f32[4,384,384]{2,1,0:T(8,128)S(1)} async-done(((f32[4,384,384]{2,1,0:T(8,128)}), f32[4,384,384]{2,1,0:T(8,128)S(1)}, u32[]{:S(2)}, u32[]{:S(2)}) %all-to-all-start) | async-done | bytes 2359328 | tf_op jit(solution)/shard_map/all_to_all | solution.py:71
  67.0 6.9 %all-to-all-start.2 = ((s32[8,1,12]{2,1,0:T(1,128)}), s32[8,1,12]{2,1,0:T(1,128)S(1)}, u32[]{:S(2)}, u32[]{:S(2)}) async-start(s32[8,1,12]{2,1,0:T(1,128)} %copy.70), calls=%async_computation.2 | async-start | bytes 8192 | tf_op jit(solution)/shard_map/all_to_all | solution.py:100
  73.9 2.9 copy.65
  76.9 2.7 dot_general.8
  79.6 14.7 %convolution_multiply_fusion = f32[16,24,1536]{2,1,0:T(8,128)S(1)} fusion(f32[16,24,1536]{2,1,0:T(8,128)S(1)} %dot_general.8, f32[1536,1536,1]{1,0,2:T(8,128)} %bitcast.64, f32[24,1536]{1,0:T(8,128)S(1)} %fusion.18), kind=kOutput, calls=%fused_computation.13 | convolution fusion | flops 10872225792 | bytes 14303232 | tf_op jit(solution)/shard_map/dot_general | solution.py:73
  94.3 13.0 %fusion.31 = f32[384,4,384]{2,0,1:T(8,128)} fusion(f32[384,1536,1]{1,0,2:T(8,128)S(1)} %bitcast.71, f32[4,384,1536]{2,1,0:T(8,128)S(1)} %bitcast.65), kind=kOutput, calls=%fused_computation.87 | convolution fusion | flops 10871635968 | bytes 14155776 | tf_op jit(solution)/shard_map/dot_general | solution.py:79
  107.3 4.8 %all-to-all-start.1 = ((f32[384,4,384]{2,0,1:T(8,128)}), f32[384,4,384]{2,0,1:T(8,128)}, u32[]{:S(2)}, u32[]{:S(2)}) async-start(f32[384,4,384]{2,0,1:T(8,128)} %fusion.31), calls=%async_computation.1 | async-start | bytes 4718592 | tf_op jit(solution)/shard_map/all_to_all | solution.py:80
  112.1 2.1 copy.78
  114.3 4.8 %gather_fusion = f32[96,4,16,384]{3,2,1,0:T(8,128)} fusion(f32[24,4,16,384]{3,2,1,0:T(8,128)S(1)} %bitcast.66, s32[1024]{0:T(1024)S(1)} %pad_clamp_fusion.1), kind=kCustom, calls=%fused_computation | custom fusion | bytes 18874752 | tf_op jit(solution)/shard_map/gather | solution.py:102
  119.1 21.3 %all-to-all-done.1 = f32[384,4,384]{2,0,1:T(8,128)} async-done(((f32[384,4,384]{2,0,1:T(8,128)}), f32[384,4,384]{2,0,1:T(8,128)}, u32[]{:S(2)}, u32[]{:S(2)}) %all-to-all-start.1) | async-done | bytes 2359328 | tf_op jit(solution)/shard_map/all_to_all | solution.py:80
  140.4 6.1 %all-to-all-start.3 = ((f32[8,12,4,16,384]{4,3,2,1,0:T(8,128)}), f32[8,12,4,16,384]{4,3,2,1,0:T(8,128)}, u32[]{:S(2)}, u32[]{:S(2)}) async-start(f32[8,12,4,16,384]{4,3,2,1,0:T(8,128)} %bitcast.67), calls=%async_computation.3 | async-start | bytes 18874368 | tf_op jit(solution)/shard_map/all_to_all | solution.py:103
  146.8 3.3 add.134
  150.1 201.9 %all-to-all-done.3 = f32[8,12,4,16,384]{4,3,2,1,0:T(8,128)} async-done(((f32[8,12,4,16,384]{4,3,2,1,0:T(8,128)}), f32[8,12,4,16,384]{4,3,2,1,0:T(8,128)}, u32[]{:S(2)}, u32[]{:S(2)}) %all-to-all-start.3) | async-done | bytes 9437216 | tf_op jit(solution)/shard_map/all_to_all | solution.py:103
  352.0 6.7 %gather_fusion.1 = f32[48,4,16,384]{3,2,1,0:T(8,128)} fusion(f32[96,4,16,384]{3,2,1,0:T(8,128)} %bitcast.20, s32[1024]{0:T(1024)S(1)} %pad_clamp_fusion), kind=kCustom, calls=%fused_computation.1 | custom fusion | bytes 9437376 | tf_op jit(solution)/shard_map/gather | solution.py:105
  358.7 2.9 fusion.2
  361.6 2.8 copy.73
  (64 shorter events, 7.8 us)
Async XLA Ops:
  0.6 9.3 %copy-start = (f32[4,16,24,384]{3,2,1,0:T(8,128)S(1)}, f32[4,16,24,384]{3,2,1,0:T(8,128)}, u32[]{:S(2)}) copy-start(f32[4,16,24,384]{3,2,1,0:T(8,128)} %param.8) | copy-start | bytes 7077892
  0.6 9.3 %copy-start.3 = (f32[16,24,384]{2,1,0:T(8,128)S(1)}, f32[16,24,384]{2,1,0:T(8,128)}, u32[]{:S(2)}) copy-start(f32[16,24,384]{2,1,0:T(8,128)} %param.11) | copy-start | bytes 1769476
  4.0 13.7 %copy-start.5 = (s32[24,2]{0,1:T(2,128)S(1)}, s32[24,2]{0,1:T(2,128)}, u32[]{:S(2)}) copy-start(s32[24,2]{0,1:T(2,128)} %param.13) | copy-start | bytes 580
  4.0 14.1 %copy-start.11 = (s32[24]{0:T(128)S(1)}, s32[24]{0:T(128)}, u32[]{:S(2)}) copy-start(s32[24]{0:T(128)} %param.12) | copy-start | bytes 292
  4.0 14.1 %copy-start.7 = (s32[24,2]{0,1:T(2,128)S(1)}, s32[24,2]{0,1:T(2,128)}, u32[]{:S(2)}) copy-start(s32[24,2]{0,1:T(2,128)} %param.14) | copy-start | bytes 580
  5.7 13.8 %collective-permute-start = (f32[5,16,24,1]{2,1,3,0:T(8,128)S(1)}, f32[5,16,24,1]{2,1,3,0:T(8,128)}, u32[]{:S(2)}, u32[]{:S(2)}) collective-permute-start(f32[5,16,24,1]{2,1,3,0:T(8,128)S(1)} %copy.57), channel_id=1, source_target_pairs={{0,8},{8,16},{16,24},{24,0},{1,9},{9,17},{17,25},{25,1},{2,10},{10... | collective-permute-start | bytes 23048 | tf_op jit(solution)/shard_map/ppermute | solution.py:17
  7.9 16.1 %collective-permute-start.1 = (f32[5,16,24,1]{2,1,3,0:T(8,128)S(1)}, f32[5,16,24,1]{2,1,3,0:T(8,128)}, u32[]{:S(2)}, u32[]{:S(2)}) collective-permute-start(f32[5,16,24,1]{2,1,3,0:T(8,128)S(1)} %copy.59), channel_id=1, source_target_pairs={{8,0},{16,8},{24,16},{0,24},{9,1},{17,9},{25,17},{1,25},{10,2},{18... | collective-permute-start | bytes 23048 | tf_op jit(solution)/shard_map/ppermute | solution.py:18
  10.8 18.3 %collective-permute-start.2 = (f32[5,16,1,384]{3,1,2,0:T(8,128)}, f32[5,16,1,384]{3,1,2,0:T(8,128)}, u32[]{:S(2)}, u32[]{:S(2)}) collective-permute-start(f32[5,16,1,384]{3,1,2,0:T(8,128)} %copy.61), channel_id=1, source_target_pairs={{0,1},{1,2},{2,3},{3,4},{4,5},{5,6},{6,7},{8,9},{9,10},{10,11},{11... | collective-permute-start | bytes 368648 | tf_op jit(solution)/shard_map/ppermute | solution.py:17
  16.3 14.1 %collective-permute-start.3 = (f32[5,16,1,384]{3,1,2,0:T(8,128)}, f32[5,16,1,384]{3,1,2,0:T(8,128)}, u32[]{:S(2)}, u32[]{:S(2)}) collective-permute-start(f32[5,16,1,384]{3,1,2,0:T(8,128)} %copy.63), channel_id=1, source_target_pairs={{1,0},{2,1},{3,2},{4,3},{5,4},{6,5},{7,6},{9,8},{10,9},{11,10},{12... | collective-permute-start | bytes 368648 | tf_op jit(solution)/shard_map/ppermute | solution.py:18
  18.0 0.6 copy-start.9
  26.3 3.8 %copy-start.4 = (f32[16,24,384]{2,1,0:T(8,128)S(1)}, f32[16,24,384]{2,1,0:T(8,128)}, u32[]{:S(2)}) copy-start(f32[16,24,384]{2,1,0:T(8,128)} %param.11) | copy-start | bytes 1769476
  30.1 1.3 copy-start.8
  34.9 32.1 %all-to-all-start = ((f32[4,384,384]{2,1,0:T(8,128)}), f32[4,384,384]{2,1,0:T(8,128)S(1)}, u32[]{:S(2)}, u32[]{:S(2)}) async-start(f32[4,384,384]{2,1,0:T(8,128)} %bitcast.68), calls=%async_computation | async-start | bytes 4718592 | tf_op jit(solution)/shard_map/all_to_all | solution.py:71
  67.0 40.3 %all-to-all-start.2 = ((s32[8,1,12]{2,1,0:T(1,128)}), s32[8,1,12]{2,1,0:T(1,128)S(1)}, u32[]{:S(2)}, u32[]{:S(2)}) async-start(s32[8,1,12]{2,1,0:T(1,128)} %copy.70), calls=%async_computation.2 | async-start | bytes 8192 | tf_op jit(solution)/shard_map/all_to_all | solution.py:100
  79.6 14.8 %copy-start.1 = (f32[24,64,1536]{2,1,0:T(8,128)S(1)}, f32[24,64,1536]{2,1,0:T(8,128)}, u32[]{:S(2)}) copy-start(f32[24,64,1536]{2,1,0:T(8,128)} %add_select_fusion) | copy-start | bytes 28311556
  107.3 33.1 %all-to-all-start.1 = ((f32[384,4,384]{2,0,1:T(8,128)}), f32[384,4,384]{2,0,1:T(8,128)}, u32[]{:S(2)}, u32[]{:S(2)}) async-start(f32[384,4,384]{2,0,1:T(8,128)} %fusion.31), calls=%async_computation.1 | async-start | bytes 4718592 | tf_op jit(solution)/shard_map/all_to_all | solution.py:80
  140.4 6.3 %copy-start.10 = (s32[48]{0:T(128)S(1)}, s32[48]{0:T(128)}, u32[]{:S(2)}) copy-start(s32[48]{0:T(128)} %copy-done.9) | copy-start | bytes 580
  140.4 6.4 %copy-start.6 = (f32[24,2]{0,1:T(2,128)S(1)}, f32[24,2]{0,1:T(2,128)}, u32[]{:S(2)}) copy-start(f32[24,2]{0,1:T(2,128)} %param.15) | copy-start | bytes 580
  140.4 6.4 %copy-start.2 = (f32[4,16,24,384]{3,2,1,0:T(8,128)S(1)}, f32[4,16,24,384]{3,2,1,0:T(8,128)}, u32[]{:S(2)}) copy-start(f32[4,16,24,384]{3,2,1,0:T(8,128)} %fusion.4) | copy-start | bytes 7077892
  140.4 211.6 %all-to-all-start.3 = ((f32[8,12,4,16,384]{4,3,2,1,0:T(8,128)}), f32[8,12,4,16,384]{4,3,2,1,0:T(8,128)}, u32[]{:S(2)}, u32[]{:S(2)}) async-start(f32[8,12,4,16,384]{4,3,2,1,0:T(8,128)} %bitcast.67), calls=%async_computation.3 | async-start | bytes 18874368 | tf_op jit(solution)/shard_map/all_to_all | solution.py:103
where the time goes:
time: 365 us; the launch traced here: 364 us
  waiting for transfers between devices  243 us (67%)
  local copies, waits for them, and re-layouts  34.2 us (9%)
  starting transfers between devices  30.1 us (8%)
  other arithmetic  28.6 us (8%)
  matrix products  27.7 us (8%)
    all_to_all x1, waiting for transfers between devices, departure_terms(): lax.all_to_all(outgoing, 'lat', split_axis=0, concat_axis=0, tiled=True)  202 us
    all_to_all x1, waiting for transfers between devices, polar_filter(): lax.all_to_all(change, 'lon', split_axis=1, concat_axis=0, tiled=True)  21.3 us
    all_to_all x1, waiting for transfers between devices, polar_filter(): lax.all_to_all(flat, 'lon', split_axis=0, concat_axis=1, tiled=True)  19.7 us
    dot_general x1, matrix products, polar_filter(): spectrum = jnp.dot(circles, basis_table, precision=PRECISE)  14.7 us
    dot_general x1, matrix products, polar_filter(): lax.dot_general(scaled, basis_table, (((1,), (1,)), ((), ())), precision=...  13 us
  transfers between devices with their start and end apart: 8, of which 3 were waited for; matrix products, arithmetic and copies ran while one was open for 19% of the time, Pallas kernels for 0%

commit v1 on v0

--- a/solution.py
+++ b/solution.py
@@ -68,7 +68,10 @@
     parts = lax.axis_size("lon")
     length = block_cells * parts
     flat = values.reshape(fields * levels * rows, block_cells)
-    circles = lax.all_to_all(flat, "lon", split_axis=0, concat_axis=1, tiled=True)
+    circles = jnp.concatenate(
+        lax.all_to_all(jnp.stack(jnp.split(flat, lax.axis_size("lon"), axis=0)), "lon", 0, 0),
+        axis=1,
+    )
     basis_table = circle_basis(length)
     spectrum = jnp.dot(circles, basis_table, precision=PRECISE)
     factors = column_factors(band_rows, length)

time: 365 us -> 367 us (level)
  no operation moved by 1% of the time
where the time goes in v1:
time: 367 us; the launch traced here: 366 us
  waiting for transfers between devices  243 us (66%)
  local copies, waits for them, and re-layouts  35.7 us (10%)
  starting transfers between devices  30.1 us (8%)
  other arithmetic  28.7 us (8%)
  matrix products  27.7 us (8%)
    all_to_all x1, waiting for transfers between devices, departure_terms(): lax.all_to_all(outgoing, 'lat', split_axis=0, concat_axis=0, tiled=True)  202 us
    all_to_all x1, waiting for transfers between devices, polar_filter(): lax.all_to_all(change, 'lon', split_axis=1, concat_axis=0, tiled=True)  21.3 us
    all_to_all x1, waiting for transfers between devices, polar_filter(): lax.all_to_all(jnp.stack(jnp.split(flat, lax.axis_size('lon'), axis=0)),...  19.7 us
    dot_general x1, matrix products, polar_filter(): spectrum = jnp.dot(circles, basis_table, precision=PRECISE)  14.7 us
    dot_general x1, matrix products, polar_filter(): lax.dot_general(scaled, basis_table, (((1,), (1,)), ((), ())), precision=...  13 us
  transfers between devices with their start and end apart: 8, of which 3 were waited for; matrix products, arithmetic and copies ran while one was open for 19% of the time, Pallas kernels for 0%

profile of v1, /device:TPU:0, one launch (start us, length us, event | category | flops | bytes accessed | tf_op | source)
XLA Modules:
  0.0 366.1 jit_solution(11269290168798170537)
XLA Ops:
  0.7 3.3 pad_maximum_fusion.9
  4.0 1.8 copy.66
  6.2 1.7 copy.68
  7.9 2.0 collective-permute-start.1
  10.7 4.9 %collective-permute-start.2 = (f32[5,16,1,384]{3,1,2,0:T(8,128)}, f32[5,16,1,384]{3,1,2,0:T(8,128)}, u32[]{:S(2)}, u32[]{:S(2)}) collective-permute-start(f32[5,16,1,384]{3,1,2,0:T(8,128)} %copy.70), channel_id=1, source_target_pairs={{0,1},{1,2},{2,3},{3,4},{4,5},{5,6},{6,7},{8,9},{9,10},{10,11},{11... | collective-permute-start | bytes 368648 | tf_op jit(solution)/shard_map/ppermute | solution.py:17
  16.2 1.3 collective-permute-start.3
  19.5 1.3 copy.67
  20.8 2.2 multiply_bitcast_fusion.1
  24.0 2.3 copy.69
  26.2 2.7 multiply_subtract_fusion
  31.4 1.2 subtract_select_fusion
  33.5 1.4 copy-done.2
  35.0 1.6 pad_maximum_fusion.8
  36.6 3.6 all-to-all-start
  41.6 1.6 fusion.14
  43.2 5.8 %add_select_fusion = f32[24,64,1536]{2,1,0:T(8,128)} fusion(f32[64,1536]{1,0:T(8,128)S(1)} %get-tuple-element.25, f32[24,1536]{1,0:T(8,128)S(1)} %get-tuple-element.23, f32[64,1536]{1,0:T(8,128)S(1)} %get-tuple-element.24, f32[24,1536]{1,0:T(8,128)S(1)} %get-tuple-element.22, pred[1536]{0:T(1024)(128)(4,1)S(1)} %iota_compare_fusion.4), kind=kLoop, calls=%fused_computation.2 | loop fusion | flops 16515072 | bytes 10520064 | tf_op jit(solution)/shard_map/jit(_where)/select_n | solution.py:62
  49.0 19.7 %all-to-all-done = f32[4,384,384]{2,1,0:T(8,128)S(1)} async-done(((f32[4,384,384]{2,1,0:T(8,128)}), f32[4,384,384]{2,1,0:T(8,128)S(1)}, u32[]{:S(2)}, u32[]{:S(2)}) %all-to-all-start) | async-done | bytes 2359328 | tf_op jit(solution)/shard_map/all_to_all | solution.py:72
  68.7 6.9 %all-to-all-start.2 = ((s32[8,1,12]{2,1,0:T(1,128)}), s32[8,1,12]{2,1,0:T(1,128)S(1)}, u32[]{:S(2)}, u32[]{:S(2)}) async-start(s32[8,1,12]{2,1,0:T(1,128)} %copy.79), calls=%async_computation.2 | async-start | bytes 8192 | tf_op jit(solution)/shard_map/all_to_all | solution.py:103
  75.6 2.9 copy.74
  78.5 2.7 dot_general.8
  81.3 14.7 %convolution_multiply_fusion = f32[16,24,1536]{2,1,0:T(8,128)S(1)} fusion(f32[16,24,1536]{2,1,0:T(8,128)S(1)} %dot_general.8, f32[1536,1536,1]{1,0,2:T(8,128)} %bitcast.67, f32[24,1536]{1,0:T(8,128)S(1)} %fusion.18), kind=kOutput, calls=%fused_computation.13 | convolution fusion | flops 10872225792 | bytes 14303232 | tf_op jit(solution)/shard_map/dot_general | solution.py:76
  96.0 13.0 %fusion.32 = f32[384,4,384]{2,0,1:T(8,128)} fusion(f32[384,1536,1]{1,0,2:T(8,128)S(1)} %bitcast.73, f32[4,384,1536]{2,1,0:T(8,128)S(1)} %bitcast.68), kind=kOutput, calls=%fused_computation.89 | convolution fusion | flops 10871635968 | bytes 14155776 | tf_op jit(solution)/shard_map/dot_general | solution.py:82
  109.0 4.8 %all-to-all-start.1 = ((f32[384,4,384]{2,0,1:T(8,128)}), f32[384,4,384]{2,0,1:T(8,128)}, u32[]{:S(2)}, u32[]{:S(2)}) async-start(f32[384,4,384]{2,0,1:T(8,128)} %fusion.32), calls=%async_computation.1 | async-start | bytes 4718592 | tf_op jit(solution)/shard_map/all_to_all | solution.py:83
  113.8 2.1 copy.87
  116.0 4.8 %gather_fusion = f32[96,4,16,384]{3,2,1,0:T(8,128)} fusion(f32[24,4,16,384]{3,2,1,0:T(8,128)S(1)} %bitcast.69, s32[1024]{0:T(1024)S(1)} %pad_clamp_fusion.1), kind=kCustom, calls=%fused_computation | custom fusion | bytes 18874752 | tf_op jit(solution)/shard_map/gather | solution.py:105
  120.8 21.3 %all-to-all-done.1 = f32[384,4,384]{2,0,1:T(8,128)} async-done(((f32[384,4,384]{2,0,1:T(8,128)}), f32[384,4,384]{2,0,1:T(8,128)}, u32[]{:S(2)}, u32[]{:S(2)}) %all-to-all-start.1) | async-done | bytes 2359328 | tf_op jit(solution)/shard_map/all_to_all | solution.py:83
  142.1 6.1 %all-to-all-start.3 = ((f32[8,12,4,16,384]{4,3,2,1,0:T(8,128)}), f32[8,12,4,16,384]{4,3,2,1,0:T(8,128)}, u32[]{:S(2)}, u32[]{:S(2)}) async-start(f32[8,12,4,16,384]{4,3,2,1,0:T(8,128)} %bitcast.70), calls=%async_computation.3 | async-start | bytes 18874368 | tf_op jit(solution)/shard_map/all_to_all | solution.py:106
  148.5 3.3 add.134
  151.8 201.9 %all-to-all-done.3 = f32[8,12,4,16,384]{4,3,2,1,0:T(8,128)} async-done(((f32[8,12,4,16,384]{4,3,2,1,0:T(8,128)}), f32[8,12,4,16,384]{4,3,2,1,0:T(8,128)}, u32[]{:S(2)}, u32[]{:S(2)}) %all-to-all-start.3) | async-done | bytes 9437216 | tf_op jit(solution)/shard_map/all_to_all | solution.py:106
  353.7 6.8 %gather_fusion.1 = f32[48,4,16,384]{3,2,1,0:T(8,128)} fusion(f32[96,4,16,384]{3,2,1,0:T(8,128)} %bitcast.23, s32[1024]{0:T(1024)S(1)} %pad_clamp_fusion), kind=kCustom, calls=%fused_computation.1 | custom fusion | bytes 9437376 | tf_op jit(solution)/shard_map/gather | solution.py:108
  360.4 2.9 fusion.2
  363.3 2.8 copy.82
  (68 shorter events, 9.8 us)
Async XLA Ops:
  0.6 9.3 %copy-start = (f32[4,16,24,384]{3,2,1,0:T(8,128)S(1)}, f32[4,16,24,384]{3,2,1,0:T(8,128)}, u32[]{:S(2)}) copy-start(f32[4,16,24,384]{3,2,1,0:T(8,128)} %param.8) | copy-start | bytes 7077892
  0.6 9.3 %copy-start.4 = (f32[16,24,384]{2,1,0:T(8,128)S(1)}, f32[16,24,384]{2,1,0:T(8,128)}, u32[]{:S(2)}) copy-start(f32[16,24,384]{2,1,0:T(8,128)} %param.11) | copy-start | bytes 1769476
  4.0 13.6 %copy-start.6 = (s32[24,2]{0,1:T(2,128)S(1)}, s32[24,2]{0,1:T(2,128)}, u32[]{:S(2)}) copy-start(s32[24,2]{0,1:T(2,128)} %param.13) | copy-start | bytes 580
  4.0 14.0 %copy-start.12 = (s32[24]{0:T(128)S(1)}, s32[24]{0:T(128)}, u32[]{:S(2)}) copy-start(s32[24]{0:T(128)} %param.12) | copy-start | bytes 292
  4.0 14.1 %copy-start.8 = (s32[24,2]{0,1:T(2,128)S(1)}, s32[24,2]{0,1:T(2,128)}, u32[]{:S(2)}) copy-start(s32[24,2]{0,1:T(2,128)} %param.14) | copy-start | bytes 580
  5.7 13.8 %collective-permute-start = (f32[5,16,24,1]{2,1,3,0:T(8,128)S(1)}, f32[5,16,24,1]{2,1,3,0:T(8,128)}, u32[]{:S(2)}, u32[]{:S(2)}) collective-permute-start(f32[5,16,24,1]{2,1,3,0:T(8,128)S(1)} %copy.66), channel_id=1, source_target_pairs={{0,8},{8,16},{16,24},{24,0},{1,9},{9,17},{17,25},{25,1},{2,10},{10... | collective-permute-start | bytes 23048 | tf_op jit(solution)/shard_map/ppermute | solution.py:17
  7.9 16.1 %collective-permute-start.1 = (f32[5,16,24,1]{2,1,3,0:T(8,128)S(1)}, f32[5,16,24,1]{2,1,3,0:T(8,128)}, u32[]{:S(2)}, u32[]{:S(2)}) collective-permute-start(f32[5,16,24,1]{2,1,3,0:T(8,128)S(1)} %copy.68), channel_id=1, source_target_pairs={{8,0},{16,8},{24,16},{0,24},{9,1},{17,9},{25,17},{1,25},{10,2},{18... | collective-permute-start | bytes 23048 | tf_op jit(solution)/shard_map/ppermute | solution.py:18
  10.7 18.3 %collective-permute-start.2 = (f32[5,16,1,384]{3,1,2,0:T(8,128)}, f32[5,16,1,384]{3,1,2,0:T(8,128)}, u32[]{:S(2)}, u32[]{:S(2)}) collective-permute-start(f32[5,16,1,384]{3,1,2,0:T(8,128)} %copy.70), channel_id=1, source_target_pairs={{0,1},{1,2},{2,3},{3,4},{4,5},{5,6},{6,7},{8,9},{9,10},{10,11},{11... | collective-permute-start | bytes 368648 | tf_op jit(solution)/shard_map/ppermute | solution.py:17
  16.2 14.1 %collective-permute-start.3 = (f32[5,16,1,384]{3,1,2,0:T(8,128)}, f32[5,16,1,384]{3,1,2,0:T(8,128)}, u32[]{:S(2)}, u32[]{:S(2)}) collective-permute-start(f32[5,16,1,384]{3,1,2,0:T(8,128)} %copy.72), channel_id=1, source_target_pairs={{1,0},{2,1},{3,2},{4,3},{5,4},{6,5},{7,6},{9,8},{10,9},{11,10},{12... | collective-permute-start | bytes 368648 | tf_op jit(solution)/shard_map/ppermute | solution.py:18
  18.0 0.6 copy-start.10
  26.2 3.8 %copy-start.5 = (f32[16,24,384]{2,1,0:T(8,128)S(1)}, f32[16,24,384]{2,1,0:T(8,128)}, u32[]{:S(2)}) copy-start(f32[16,24,384]{2,1,0:T(8,128)} %param.11) | copy-start | bytes 1769476
  30.1 1.3 copy-start.9
  33.4 1.4 copy-start.2
  36.6 32.1 %all-to-all-start = ((f32[4,384,384]{2,1,0:T(8,128)}), f32[4,384,384]{2,1,0:T(8,128)S(1)}, u32[]{:S(2)}, u32[]{:S(2)}) async-start(f32[4,384,384]{2,1,0:T(8,128)} %pad_maximum_fusion.8), calls=%async_computation | async-start | bytes 4718592 | tf_op jit(solution)/shard_map/all_to_all | solution.py:72
  68.7 40.3 %all-to-all-start.2 = ((s32[8,1,12]{2,1,0:T(1,128)}), s32[8,1,12]{2,1,0:T(1,128)S(1)}, u32[]{:S(2)}, u32[]{:S(2)}) async-start(s32[8,1,12]{2,1,0:T(1,128)} %copy.79), calls=%async_computation.2 | async-start | bytes 8192 | tf_op jit(solution)/shard_map/all_to_all | solution.py:103
  81.3 14.8 %copy-start.1 = (f32[24,64,1536]{2,1,0:T(8,128)S(1)}, f32[24,64,1536]{2,1,0:T(8,128)}, u32[]{:S(2)}) copy-start(f32[24,64,1536]{2,1,0:T(8,128)} %add_select_fusion) | copy-start | bytes 28311556
  109.0 33.1 %all-to-all-start.1 = ((f32[384,4,384]{2,0,1:T(8,128)}), f32[384,4,384]{2,0,1:T(8,128)}, u32[]{:S(2)}, u32[]{:S(2)}) async-start(f32[384,4,384]{2,0,1:T(8,128)} %fusion.32), calls=%async_computation.1 | async-start | bytes 4718592 | tf_op jit(solution)/shard_map/all_to_all | solution.py:83
  142.1 6.3 %copy-start.11 = (s32[48]{0:T(128)S(1)}, s32[48]{0:T(128)}, u32[]{:S(2)}) copy-start(s32[48]{0:T(128)} %copy-done.10) | copy-start | bytes 580
  142.1 6.4 %copy-start.7 = (f32[24,2]{0,1:T(2,128)S(1)}, f32[24,2]{0,1:T(2,128)}, u32[]{:S(2)}) copy-start(f32[24,2]{0,1:T(2,128)} %param.15) | copy-start | bytes 580
  142.1 6.4 %copy-start.3 = (f32[4,16,24,384]{3,2,1,0:T(8,128)S(1)}, f32[4,16,24,384]{3,2,1,0:T(8,128)}, u32[]{:S(2)}) copy-start(f32[4,16,24,384]{3,2,1,0:T(8,128)} %copy-done.2) | copy-start | bytes 7077892
  142.1 211.6 %all-to-all-start.3 = ((f32[8,12,4,16,384]{4,3,2,1,0:T(8,128)}), f32[8,12,4,16,384]{4,3,2,1,0:T(8,128)}, u32[]{:S(2)}, u32[]{:S(2)}) async-start(f32[8,12,4,16,384]{4,3,2,1,0:T(8,128)} %bitcast.70), calls=%async_computation.3 | async-start | bytes 18874368 | tf_op jit(solution)/shard_map/all_to_all | solution.py:106
